TPU v7x, 256 devices: a whole 4x4x8 slice. The times are simulated.
256 devices in a mesh: seq: 32 (over z, y), tp: 8 (over x, core).
Axes of the slice: x: 4, y: 4, z: 8, core: 2. Of those that a mesh axis runs over, the one named last changes fastest.
Arguments:
- tokens: bfloat16 [384, 4096], P(None, 'seq'), may hold values from -30 to 30
- ln_first_gain: bfloat16 [4096], P('seq'), may hold values from 0.099609375 to 1.8984375
- w_qkv: bfloat16 [4096, 3, 4096], P('seq', None, 'tp'), may hold values from -0.25 to 0.25
- w_out: bfloat16 [4096, 4096], P('tp', 'seq'), may hold values from -1 to 1
- ln_second_gain: bfloat16 [4096], P('seq'), may hold values from 0.099609375 to 1.8984375
- w_up: bfloat16 [4096, 16384], P('seq', 'tp'), may hold values from -0.09375 to 0.09375
- w_down: bfloat16 [16384, 4096], P('tp', 'seq'), may hold values from -0.09375 to 0.09375
- prompt_key: bfloat16 [8, 16384, 4096], P(None, 'seq', 'tp'), may hold values from -200 to 200
- prompt_val: bfloat16 [8, 16384, 4096], P(None, 'seq', 'tp'), may hold values from -20 to 20
- cont_key: bfloat16 [96, 256, 4096], P('seq', None, 'tp'), may hold values from -18 to 18
- cont_val: bfloat16 [96, 256, 4096], P('seq', None, 'tp'), may hold values from -20 to 20
- group_ids: int32 [96], replicated, may hold values from 0 to 7, as said below
- prompt_len: int32 [8], replicated, may hold values from 1 to 16384, as said below
- cont_len: int32 [96], replicated, may hold values from 0 to 252, as said below
Outputs:
- layer_out: bfloat16 [384, 4096], P(None, 'seq')
Inputs may be any that keep to these rules, and one draw needn't show every extreme that they name: `group_ids`: each of the 8 groups is named by exactly 12 requests. `prompt_len`: one group's prompt has exactly 16384 positions. `cont_len`: some request has exactly 252 filled slots.
All inputs are finite; a program needn't handle non-finite values.
Results may differ from a plain program's by a relative error of at most 0.013.
The roundings to bfloat16 on the way count: a program that leaves them out, or rounds other values in their place, can miss the bound.
Values may be sent and summed in bfloat16 or wider, within the bound.
No kernel may reach another device: no remote copies, remote signals or barrier semaphores. Data moves between devices by JAX's collectives and lax.ppermute only.
A program may use at most 128 MiB of HBM per device.

v0:
```python
import math

import jax
import jax.numpy as jnp
from jax import lax
from jax.sharding import PartitionSpec as P

D = 4096
HEADS = 32
HD = 128
NEW = 4


NEG_FILL = -1e30
NORM_EPS = 1e-05


def finish_norm(values, row_sum, row_square, gain):
    mean_row = row_sum / D
    variance = row_square / D - mean_row * mean_row
    scaled = (values - mean_row[:, None]) * lax.rsqrt(variance + NORM_EPS)[:, None]
    return (scaled * gain.astype(jnp.float32)[None, :]).astype(jnp.bfloat16)


def combine_parts(earlier, later):
    merged_top = jnp.maximum(earlier[0], later[0])
    left_factor = jnp.exp(earlier[0] - merged_top)
    right_factor = jnp.exp(later[0] - merged_top)
    merged_sum = earlier[1] * left_factor + later[1] * right_factor
    merged_acc = earlier[2] * left_factor[..., None] + later[2] * right_factor[..., None]
    return (merged_top, merged_sum, merged_acc)


def body(
    tokens,
    ln_first_gain,
    w_qkv,
    w_out,
    ln_second_gain,
    w_up,
    w_down,
    prompt_key,
    prompt_val,
    cont_key,
    cont_val,
    group_ids,
    prompt_len,
    cont_len,
):
    row_count = tokens.shape[0]
    seq_index = lax.axis_index("seq")
    tp_index = lax.axis_index("tp")
    feat_width = w_qkv.shape[2]
    local_heads = feat_width // HD
    home_requests = cont_key.shape[0]
    home_rows = home_requests * NEW
    requests = row_count // NEW
    groups = prompt_key.shape[0]
    block_len = prompt_key.shape[1]
    slots = cont_key.shape[1]
    score_scale = 1.0 / math.sqrt(HD)
    token_float = tokens.astype(jnp.float32)
    first_sums = lax.psum((jnp.sum(token_float, 1), jnp.sum(token_float * token_float, 1)), "seq")
    normed = finish_norm(token_float, first_sums[0], first_sums[1], ln_first_gain)
    w_flat = w_qkv.reshape(w_qkv.shape[0], 3 * feat_width)
    partial_qkv = jnp.dot(normed, w_flat, preferred_element_type=jnp.float32)
    full_qkv = lax.psum(partial_qkv, "seq").astype(jnp.bfloat16)
    query = full_qkv[:, :feat_width]
    own_slice = lax.dynamic_slice_in_dim(full_qkv, seq_index * home_rows, home_rows, 0)
    key_new = own_slice[:, feat_width : 2 * feat_width]
    val_new = own_slice[:, 2 * feat_width :]
    head_first = (tp_index * local_heads).astype(jnp.float32)
    slopes = jnp.exp2(
        -8.0 * (head_first + jnp.arange(local_heads, dtype=jnp.float32) + 1.0) / HEADS
    )
    members = jnp.argsort(group_ids, stable=True).reshape(groups, requests // groups)
    inverse = jnp.argsort(members.reshape(-1))
    group_match = group_ids[:, None] == jnp.arange(groups, dtype=jnp.int32)[None, :]
    req_prompt = jnp.sum(jnp.where(group_match, prompt_len[None, :], 0), 1)
    query_pos = (req_prompt + cont_len)[:, None] + jnp.arange(NEW, dtype=jnp.int32)[None, :]
    query_req = query.reshape(requests, NEW, local_heads, HD)
    group_query = query_req[members].reshape(groups, -1, local_heads, HD)
    group_pos = query_pos[members].reshape(groups, -1)
    key_slab = prompt_key.reshape(groups, block_len, local_heads, HD)
    val_slab = prompt_val.reshape(groups, block_len, local_heads, HD)
    key_pos = seq_index * block_len + jnp.arange(block_len, dtype=jnp.int32)
    scores = jnp.einsum(
        "gqhd,gphd->ghqp", group_query, key_slab, preferred_element_type=jnp.float32
    )
    distance = (key_pos[None, None, :] - group_pos[:, :, None]).astype(jnp.float32)
    scores = scores * score_scale + slopes[None, :, None, None] * distance[:, None, :, :]
    is_live = (key_pos[None, :] < prompt_len[:, None])[:, None, None, :]
    block_top = jnp.max(jnp.where(is_live, scores, NEG_FILL), -1)
    weights = jnp.where(is_live, jnp.exp(scores - block_top[..., None]), 0.0)
    block_sum = jnp.sum(weights, -1)
    block_acc = jnp.einsum(
        "ghqp,gphd->gqhd",
        weights.astype(jnp.bfloat16),
        val_slab,
        preferred_element_type=jnp.float32,
    )
    prompt_top = (
        jnp.transpose(block_top, (0, 2, 1))
        .reshape(requests, NEW, local_heads)[inverse]
        .reshape(row_count, local_heads)
    )
    prompt_sum = (
        jnp.transpose(block_sum, (0, 2, 1))
        .reshape(requests, NEW, local_heads)[inverse]
        .reshape(row_count, local_heads)
    )
    prompt_acc = block_acc.reshape(requests, NEW, local_heads, HD)[inverse].reshape(
        row_count, local_heads, HD
    )
    home_query = lax.dynamic_slice_in_dim(query_req, seq_index * home_requests, home_requests, 0)
    home_pos = lax.dynamic_slice_in_dim(query_pos, seq_index * home_requests, home_requests, 0)
    home_prompt = lax.dynamic_slice_in_dim(req_prompt, seq_index * home_requests, home_requests, 0)
    home_filled = lax.dynamic_slice_in_dim(cont_len, seq_index * home_requests, home_requests, 0)
    cache_keys = cont_key.reshape(home_requests, slots, local_heads, HD)
    cache_vals = cont_val.reshape(home_requests, slots, local_heads, HD)
    slot_index = jnp.arange(slots, dtype=jnp.int32)
    cache_pos = home_prompt[:, None] + slot_index[None, :]
    cache_scores = (
        jnp.einsum("rjhd,rkhd->rhjk", home_query, cache_keys, preferred_element_type=jnp.float32)
        * score_scale
    )
    cache_scores = cache_scores + slopes[None, :, None, None] * (
        cache_pos[:, None, None, :] - home_pos[:, None, :, None]
    ).astype(jnp.float32)
    cache_live = (slot_index[None, :] < home_filled[:, None])[:, None, None, :]
    fresh_keys = key_new.reshape(home_requests, NEW, local_heads, HD)
    fresh_vals = val_new.reshape(home_requests, NEW, local_heads, HD)
    steps_new = jnp.arange(NEW, dtype=jnp.int32)
    fresh_dist = (steps_new[None, :] - steps_new[:, None]).astype(jnp.float32)
    fresh_scores = (
        jnp.einsum("rjhd,rkhd->rhjk", home_query, fresh_keys, preferred_element_type=jnp.float32)
        * score_scale
    )
    fresh_scores = fresh_scores + slopes[None, :, None, None] * fresh_dist[None, None, :, :]
    fresh_live = (steps_new[None, :] <= steps_new[:, None])[None, None, :, :]
    home_top = jnp.maximum(
        jnp.max(jnp.where(cache_live, cache_scores, NEG_FILL), -1),
        jnp.max(jnp.where(fresh_live, fresh_scores, NEG_FILL), -1),
    )
    cache_weights = jnp.where(cache_live, jnp.exp(cache_scores - home_top[..., None]), 0.0)
    fresh_weights = jnp.where(fresh_live, jnp.exp(fresh_scores - home_top[..., None]), 0.0)
    home_sum = jnp.sum(cache_weights, -1) + jnp.sum(fresh_weights, -1)
    home_acc = jnp.einsum(
        "rhjk,rkhd->rjhd",
        cache_weights.astype(jnp.bfloat16),
        cache_vals,
        preferred_element_type=jnp.float32,
    )
    home_acc = home_acc + jnp.einsum(
        "rhjk,rkhd->rjhd",
        fresh_weights.astype(jnp.bfloat16),
        fresh_vals,
        preferred_element_type=jnp.float32,
    )
    home_top = jnp.transpose(home_top, (0, 2, 1)).reshape(home_rows, local_heads)
    home_sum = jnp.transpose(home_sum, (0, 2, 1)).reshape(home_rows, local_heads)
    home_acc = home_acc.reshape(home_rows, local_heads, HD)
    row_start = seq_index * home_rows
    home_part = (
        lax.dynamic_update_slice_in_dim(
            jnp.full((row_count, local_heads), NEG_FILL, jnp.float32), home_top, row_start, 0
        ),
        lax.dynamic_update_slice_in_dim(
            jnp.zeros((row_count, local_heads), jnp.float32), home_sum, row_start, 0
        ),
        lax.dynamic_update_slice_in_dim(
            jnp.zeros((row_count, local_heads, HD), jnp.float32), home_acc, row_start, 0
        ),
    )
    local_part = combine_parts((prompt_top, prompt_sum, prompt_acc), home_part)
    global_top = lax.pmax(local_part[0], "seq")
    factor = jnp.exp(local_part[0] - global_top)
    merged_sum, merged_acc = lax.psum(
        (local_part[1] * factor, local_part[2] * factor[..., None]), "seq"
    )
    attended = (
        (merged_acc / merged_sum[..., None]).reshape(row_count, feat_width).astype(jnp.bfloat16)
    )
    attn_sum = lax.psum(jnp.dot(attended, w_out, preferred_element_type=jnp.float32), "tp")
    hidden_state = token_float + attn_sum
    second_sums = lax.psum(
        (jnp.sum(hidden_state, 1), jnp.sum(hidden_state * hidden_state, 1)), "seq"
    )
    second_normed = finish_norm(hidden_state, second_sums[0], second_sums[1], ln_second_gain)
    up_sum = lax.psum(jnp.dot(second_normed, w_up, preferred_element_type=jnp.float32), "seq")
    activated = jax.nn.gelu(up_sum, approximate=False).astype(jnp.bfloat16)
    down_part = jnp.dot(activated, w_down, preferred_element_type=jnp.float32)
    down_sum = lax.psum(down_part.astype(jnp.bfloat16), "tp").astype(jnp.float32)
    return (hidden_state + down_sum).astype(jnp.bfloat16)


def solution(mesh):
    in_specs = (
        P(None, "seq"),
        P("seq"),
        P("seq", None, "tp"),
        P("tp", "seq"),
        P("seq"),
        P("seq", "tp"),
        P("tp", "seq"),
        P(None, "seq", "tp"),
        P(None, "seq", "tp"),
        P("seq", None, "tp"),
        P("seq", None, "tp"),
        P(),
        P(),
        P(),
    )
    out_specs = P(None, "seq")
    return jax.shard_map(body, mesh=mesh, in_specs=in_specs, out_specs=out_specs, check_vma=False)
```

profile of v0, /device:TPU:16, one launch (start us, length us, event | category | flops | bytes accessed | tf_op | source)
XLA Modules:
  0.0 878.5 jit_solution(7815176637591646648)
XLA Ops:
  6.6 0.8 select_reduce_fusion.3
  7.4 0.6 dynamic_slice.17
  8.0 0.7 add.155
  8.7 1.3 dynamic_slice.15
  9.9 1.2 convert_element_type.71
  11.2 3.2 sort.34
  14.4 0.5 copy-done.5
  15.1 1.1 convert_reduce_fusion
  16.3 1.2 gather_fusion.1
  17.5 1.2 copy.124
  18.7 73.5 %all-reduce.1 = (f32[384]{0:T(512)S(1)}, f32[384]{0:T(512)S(1)}) all-reduce(f32[384]{0:T(512)S(1)} %get-tuple-element.12, f32[384]{0:T(512)S(1)} %get-tuple-element.11), channel_id=1, replica_groups=mesh['seq'=32,'tp'=8] {'seq'}, use_global_device_ids=true, to_apply=%region_3.0 | all-reduce | flops 768 | bytes 6144 | tf_op jit(solution)/shard_map/psum | solution.py:63
  92.2 1.4 fusion.48
  93.6 163.9 %all-reduce.15 = bf16[384,1536]{1,0:T(8,128)(2,1)} all-reduce(f32[384,1536]{1,0:T(8,128)S(1)} %fusion.48), channel_id=1, replica_groups=mesh['seq'=32,'tp'=8] {'seq'}, use_global_device_ids=true, to_apply=%region_4.0 | all-reduce | flops 589824 | bytes 3538944 | tf_op jit(solution)/shard_map/psum | solution.py:67
  257.5 1.1 slice.22
  258.7 0.9 gather_fusion
  259.7 0.7 iota_compare_fusion
  260.4 3.2 sort.35
  263.6 0.7 iota_add_fusion.1
  264.3 0.7 broadcast_compare_fusion
  265.0 0.9 sub.109
  266.0 0.9 fusion.107
  267.2 0.4 select_reduce_fusion.1
  267.9 0.3 convolution_bitcast_fusion.1
  268.1 0.2 fusion.36
  268.6 4.0 select_reduce_fusion
  272.6 1.1 fusion.16
  273.7 1.5 fusion.27
  275.3 1.1 gather_fusion.2
  276.7 0.7 gather_fusion.4
  277.7 0.7 gather_fusion.3
  278.5 0.3 dynamic_update_slice.9
  278.8 72.8 %pmax.7 = f32[384,4]{0,1:T(4,128)S(1)} all-reduce(f32[384,4]{0,1:T(4,128)S(1)} %max.18), channel_id=1, replica_groups=mesh['seq'=32,'tp'=8] {'seq'}, use_global_device_ids=true, to_apply=%region_11.12 | all-reduce | flops 1536 | bytes 12288 | tf_op jit(solution)/shard_map/pmax | solution.py:176
  351.6 0.3 dynamic_update_slice.11
  352.2 1.5 add_multiply_fusion
  353.8 70.7 %psum.74 = f32[384,4]{0,1:T(4,128)S(1)} all-reduce(f32[384,4]{0,1:T(4,128)S(1)} %get-tuple-element.17), channel_id=1, replica_groups=mesh['seq'=32,'tp'=8] {'seq'}, use_global_device_ids=true, to_apply=%region_16.17 | all-reduce | flops 1536 | bytes 12288 | tf_op jit(solution)/shard_map/psum | solution.py:178
  424.6 76.9 %all-reduce.8.cloned.1.call-done = f32[384,4,128]{2,0,1:T(8,128)} async-done(((f32[384,4,128]{2,0,1:T(8,128)}), f32[384,4,128]{2,0,1:T(8,128)}) %all-reduce.8.cloned.1.call-update) | async-done | bytes 786448 | tf_op jit(solution)/shard_map/psum | solution.py:178
  501.4 1.4 divide_convert_fusion
  502.8 0.2 copy.147
  503.1 1.0 fusion.108
  504.1 64.2 %all-reduce.10.cloned.1.call-done = f32[384,128]{1,0:T(8,128)} async-done(((f32[384,128]{1,0:T(8,128)}), f32[384,128]{1,0:T(8,128)}) %all-reduce.10.cloned.1.call-update) | async-done | bytes 196624 | tf_op jit(solution)/shard_map/psum | solution.py:184
  568.3 1.1 fusion.64
  569.4 70.8 %all-reduce = (f32[384]{0:T(512)S(1)}, f32[384]{0:T(512)S(1)}) all-reduce(f32[384]{0:T(512)S(1)} %get-tuple-element.10, f32[384]{0:T(512)S(1)} %get-tuple-element.9), channel_id=1, replica_groups=mesh['seq'=32,'tp'=8] {'seq'}, use_global_device_ids=true, to_apply=%region_21.22 | all-reduce | flops 768 | bytes 6144 | tf_op jit(solution)/shard_map/psum | solution.py:186
  640.3 3.3 fusion.47
  643.7 0.2 all-reduce.14.cloned.1.call-start
  643.9 155.0 %all-reduce.12.cloned.1.call-done = f32[384,2048]{1,0:T(8,128)} async-done(((f32[384,2048]{1,0:T(8,128)}), f32[384,2048]{1,0:T(8,128)}) %all-reduce.12.cloned.1.call-update) | async-done | bytes 3145744 | tf_op jit(solution)/shard_map/psum | solution.py:190
  798.9 9.0 %fusion.32 = bf16[384,128]{1,0:T(8,128)(2,1)} fusion(bf16[2048,128]{1,0:T(8,128)(2,1)S(1)} %copy-done.8, f32[384,2048]{1,0:T(8,128)} %all-reduce.12.cloned.1.call-done), kind=kOutput, calls=%fused_computation.43 | convolution fusion | flops 252493824 | bytes 3768320 | tf_op jit(solution)/shard_map/dot_general | solution.py:192
  807.9 62.4 %all-reduce.14.cloned.1.call-done = bf16[384,128]{1,0:T(8,128)(2,1)} async-done(((bf16[384,128]{1,0:T(8,128)(2,1)}), bf16[384,128]{1,0:T(8,128)(2,1)}) %all-reduce.14.cloned.1.call-update) | async-done | bytes 98320 | tf_op jit(solution)/shard_map/psum | solution.py:193
  870.4 1.6 add_convert_fusion
  (73 shorter events, 2.5 us)
Async XLA Ops:
  6.5 260.7 %copy-start = (bf16[3,256,512]{2,1,0:T(8,128)(2,1)S(1)}, bf16[3,256,512]{2,1,0:T(8,128)(2,1)}, u32[]{:S(2)}) copy-start(bf16[3,256,512]{2,1,0:T(8,128)(2,1)} %param.23) | copy-start | bytes 2359300
  6.5 494.9 %all-reduce.8.cloned.1.call-start = ((), (), s32[]{:S(2)}) async-start(), calls=%async_computation | async-start | bytes 1572864 | tf_op jit(solution)/shard_map/psum | solution.py:178
  14.4 0.5 copy-start.5
  257.5 10.4 %copy-start.7 = (bf16[3,256,512]{2,1,0:T(8,128)(2,1)S(1)}, bf16[3,256,512]{2,1,0:T(8,128)(2,1)}, u32[]{:S(2)}) copy-start(bf16[3,256,512]{2,1,0:T(8,128)(2,1)} %param.24) | copy-start | bytes 2359300
  268.6 5.1 copy-start.6
  278.4 224.6 %copy-start.4 = (bf16[512,128]{1,0:T(8,128)(2,1)S(1)}, bf16[512,128]{1,0:T(8,128)(2,1)}, u32[]{:S(2)}) copy-start(bf16[512,128]{1,0:T(8,128)(2,1)} %param.17) | copy-start | bytes 393220
  351.9 152.2 %copy-start.9 = (bf16[128]{0:T(256)(128)(2,1)S(1)}, bf16[128]{0:T(256)(128)(2,1)}, u32[]{:S(2)}) copy-start(bf16[128]{0:T(256)(128)(2,1)} %param.18) | copy-start | bytes 772
  351.9 216.4 %copy-start.1 = (bf16[384,128]{1,0:T(8,128)(2,1)S(1)}, bf16[384,128]{1,0:T(8,128)(2,1)}, u32[]{:S(2)}) copy-start(bf16[384,128]{1,0:T(8,128)(2,1)} %param.14) | copy-start | bytes 294916
  352.2 288.1 %copy-start.3 = (bf16[128,2048]{1,0:T(8,128)(2,1)S(1)}, bf16[128,2048]{1,0:T(8,128)(2,1)}, u32[]{:S(2)}) copy-start(bf16[128,2048]{1,0:T(8,128)(2,1)} %param.19) | copy-start | bytes 1572868
  353.8 214.6 %all-reduce.10.cloned.1.call-start = ((), (), s32[]{:S(2)}) async-start(), calls=%async_computation.1 | async-start | bytes 393216 | tf_op jit(solution)/shard_map/psum | solution.py:184
  504.1 294.8 %all-reduce.12.cloned.1.call-start = ((), (), s32[]{:S(2)}) async-start(), calls=%async_computation.2 | async-start | bytes 6291456 | tf_op jit(solution)/shard_map/psum | solution.py:190
  640.3 158.6 %copy-start.8 = (bf16[2048,128]{1,0:T(8,128)(2,1)S(1)}, bf16[2048,128]{1,0:T(8,128)(2,1)}, u32[]{:S(2)}) copy-start(bf16[2048,128]{1,0:T(8,128)(2,1)} %param.20) | copy-start | bytes 1572868
  643.7 226.7 %copy-start.2 = (f32[384,128]{1,0:T(8,128)S(1)}, f32[384,128]{1,0:T(8,128)}, u32[]{:S(2)}) copy-start(f32[384,128]{1,0:T(8,128)} %all-reduce.10.cloned.1.call-done) | copy-start | bytes 589828
  643.7 226.7 %all-reduce.14.cloned.1.call-start = ((), (), s32[]{:S(2)}) async-start(), calls=%async_computation.3 | async-start | bytes 196608 | tf_op jit(solution)/shard_map/psum | solution.py:193
Sparse Core Ops, SparseCore 0:
  353.9 147.4 all-reduce.7
  504.2 64.1 all-reduce.9
  643.8 155.0 all-reduce.11
  808.0 62.2 all-reduce.13
where the time goes:
time: 879 us; the launch traced here: 878 us
  blocking collectives  452 us (51%)
  waiting for transfers between devices  359 us (41%)
  matrix products  21.3 us (2%)
  other arithmetic  19.7 us (2%)
  between operations  13.5 us (2%)
  local copies, waits for them, and re-layouts  13.4 us (2%)
    psum x1, blocking collectives, body(): full_qkv = lax.psum(partial_qkv, 'seq').astype(jnp.bfloat16)  164 us
    psum x1, waiting for transfers between devices, body(): lax.psum(jnp.dot(second_normed, w_up, preferred_element_type=jnp.float32)...  155 us
    psum x1, waiting for transfers between devices, body(): lax.psum((local_part[1] * factor, local_part[2] * factor[..., None]), 'seq')  76.9 us
    psum x1, blocking collectives, body(): lax.psum((jnp.sum(token_float, 1), jnp.sum(token_float * token_float, 1))...  73.5 us
    pmax x1, blocking collectives, body(): global_top = lax.pmax(local_part[0], 'seq')  72.8 us
    psum x1, blocking collectives, body(): lax.psum((jnp.sum(hidden_state, 1), jnp.sum(hidden_state * hidden_state,...  70.8 us
    psum x1, blocking collectives, body(): lax.psum((local_part[1] * factor, local_part[2] * factor[..., None]), 'seq')  70.7 us
    psum x1, waiting for transfers between devices, body(): lax.psum(jnp.dot(attended, w_out, preferred_element_type=jnp.float32), 'tp')  64.2 us
  transfers between devices with their start and end apart: 4, of which 4 were waited for; matrix products, arithmetic and copies ran while one was open for 0% of the time, Pallas kernels for 0%

commit v1 on v0

--- a/solution.py
+++ b/solution.py
@@ -29,6 +29,63 @@
     merged_sum = earlier[1] * left_factor + later[1] * right_factor
     merged_acc = earlier[2] * left_factor[..., None] + later[2] * right_factor[..., None]
     return (merged_top, merged_sum, merged_acc)
+
+
+def _levels(n):
+    return n.bit_length() - 1
+
+
+def _pairs(n, bit):
+    return [(i, i ^ (1 << bit)) for i in range(n)]
+
+
+def ar_doubling(x, axis, n, order):
+    for bit in order:
+        x = x + lax.ppermute(x, axis, _pairs(n, bit))
+    return x
+
+
+def add_parts(keep, got):
+    return tuple(a + b for a, b in zip(keep, got))
+
+
+def rs_halving(parts, axis, n, order, index, merge):
+    levels = _levels(n)
+    parts = tuple(p.reshape((2,) * levels + (p.shape[0] // n,) + p.shape[1:]) for p in parts)
+    remaining = list(range(levels - 1, -1, -1))
+    for bit in order:
+        ax = remaining.index(bit)
+        mine = (index >> bit) & 1
+        keep = tuple(lax.dynamic_index_in_dim(p, mine, ax, keepdims=False) for p in parts)
+        send = tuple(lax.dynamic_index_in_dim(p, 1 - mine, ax, keepdims=False) for p in parts)
+        got = lax.ppermute(send, axis, _pairs(n, bit))
+        parts = merge(keep, got)
+        remaining.remove(bit)
+    return parts
+
+
+def ag_doubling(x, axis, n, order, index):
+    levels = _levels(n)
+    have = []
+    for bit in order:
+        got = lax.ppermute(x, axis, _pairs(n, bit))
+        first = ((index >> bit) & 1) == 0
+        low = jnp.where(first, x, got)
+        high = jnp.where(first, got, x)
+        pos = sum(1 for b in have if b > bit)
+        x = jnp.stack([low, high], axis=pos)
+        have.insert(pos, bit)
+    return x.reshape((-1,) + x.shape[levels + 1 :])
+
+
+def seq_orders(n):
+    levels = _levels(n)
+    near = [b for b in (0, 2, 1, 3, 4) if b < levels] + list(range(5, levels))
+    return near, near[::-1]
+
+
+def tp_order(n):
+    return list(range(_levels(n)))
 
 
 def body(
@@ -50,6 +107,10 @@
     row_count = tokens.shape[0]
     seq_index = lax.axis_index("seq")
     tp_index = lax.axis_index("tp")
+    n_seq = lax.axis_size("seq")
+    n_tp = lax.axis_size("tp")
+    halve_order, double_order = seq_orders(n_seq)
+    tp_bits = tp_order(n_tp)
     feat_width = w_qkv.shape[2]
     local_heads = feat_width // HD
     home_requests = cont_key.shape[0]
@@ -60,15 +121,18 @@
     slots = cont_key.shape[1]
     score_scale = 1.0 / math.sqrt(HD)
     token_float = tokens.astype(jnp.float32)
-    first_sums = lax.psum((jnp.sum(token_float, 1), jnp.sum(token_float * token_float, 1)), "seq")
-    normed = finish_norm(token_float, first_sums[0], first_sums[1], ln_first_gain)
+    first_stats = ar_doubling(
+        jnp.stack([jnp.sum(token_float, 1), jnp.sum(token_float * token_float, 1)]),
+        "seq", n_seq, halve_order,
+    )
+    normed = finish_norm(token_float, first_stats[0], first_stats[1], ln_first_gain)
     w_flat = w_qkv.reshape(w_qkv.shape[0], 3 * feat_width)
     partial_qkv = jnp.dot(normed, w_flat, preferred_element_type=jnp.float32)
-    full_qkv = lax.psum(partial_qkv, "seq").astype(jnp.bfloat16)
-    query = full_qkv[:, :feat_width]
-    own_slice = lax.dynamic_slice_in_dim(full_qkv, seq_index * home_rows, home_rows, 0)
-    key_new = own_slice[:, feat_width : 2 * feat_width]
-    val_new = own_slice[:, 2 * feat_width :]
+    (own_qkv,) = rs_halving((partial_qkv,), "seq", n_seq, halve_order, seq_index, add_parts)
+    own_qkv = own_qkv.astype(jnp.bfloat16)
+    query = ag_doubling(own_qkv[:, :feat_width], "seq", n_seq, double_order, seq_index)
+    key_new = own_qkv[:, feat_width : 2 * feat_width]
+    val_new = own_qkv[:, 2 * feat_width :]
     head_first = (tp_index * local_heads).astype(jnp.float32)
     slopes = jnp.exp2(
         -8.0 * (head_first + jnp.arange(local_heads, dtype=jnp.float32) + 1.0) / HEADS
@@ -112,6 +176,9 @@
     prompt_acc = block_acc.reshape(requests, NEW, local_heads, HD)[inverse].reshape(
         row_count, local_heads, HD
     )
+    own_prompt = rs_halving(
+        (prompt_top, prompt_sum, prompt_acc), "seq", n_seq, halve_order, seq_index, combine_parts
+    )
     home_query = lax.dynamic_slice_in_dim(query_req, seq_index * home_requests, home_requests, 0)
     home_pos = lax.dynamic_slice_in_dim(query_pos, seq_index * home_requests, home_requests, 0)
     home_prompt = lax.dynamic_slice_in_dim(req_prompt, seq_index * home_requests, home_requests, 0)
@@ -160,37 +227,26 @@
     home_top = jnp.transpose(home_top, (0, 2, 1)).reshape(home_rows, local_heads)
     home_sum = jnp.transpose(home_sum, (0, 2, 1)).reshape(home_rows, local_heads)
     home_acc = home_acc.reshape(home_rows, local_heads, HD)
-    row_start = seq_index * home_rows
-    home_part = (
-        lax.dynamic_update_slice_in_dim(
-            jnp.full((row_count, local_heads), NEG_FILL, jnp.float32), home_top, row_start, 0
-        ),
-        lax.dynamic_update_slice_in_dim(
-            jnp.zeros((row_count, local_heads), jnp.float32), home_sum, row_start, 0
-        ),
-        lax.dynamic_update_slice_in_dim(
-            jnp.zeros((row_count, local_heads, HD), jnp.float32), home_acc, row_start, 0
-        ),
-    )
-    local_part = combine_parts((prompt_top, prompt_sum, prompt_acc), home_part)
-    global_top = lax.pmax(local_part[0], "seq")
-    factor = jnp.exp(local_part[0] - global_top)
-    merged_sum, merged_acc = lax.psum(
-        (local_part[1] * factor, local_part[2] * factor[..., None]), "seq"
-    )
-    attended = (
-        (merged_acc / merged_sum[..., None]).reshape(row_count, feat_width).astype(jnp.bfloat16)
-    )
-    attn_sum = lax.psum(jnp.dot(attended, w_out, preferred_element_type=jnp.float32), "tp")
+    merged = combine_parts(own_prompt, (home_top, home_sum, home_acc))
+    own_attended = (
+        (merged[2] / merged[1][..., None]).reshape(home_rows, feat_width).astype(jnp.bfloat16)
+    )
+    attended = ag_doubling(own_attended, "seq", n_seq, double_order, seq_index)
+    attn_sum = ar_doubling(
+        jnp.dot(attended, w_out, preferred_element_type=jnp.float32), "tp", n_tp, tp_bits
+    )
     hidden_state = token_float + attn_sum
-    second_sums = lax.psum(
-        (jnp.sum(hidden_state, 1), jnp.sum(hidden_state * hidden_state, 1)), "seq"
-    )
-    second_normed = finish_norm(hidden_state, second_sums[0], second_sums[1], ln_second_gain)
-    up_sum = lax.psum(jnp.dot(second_normed, w_up, preferred_element_type=jnp.float32), "seq")
-    activated = jax.nn.gelu(up_sum, approximate=False).astype(jnp.bfloat16)
+    second_stats = ar_doubling(
+        jnp.stack([jnp.sum(hidden_state, 1), jnp.sum(hidden_state * hidden_state, 1)]),
+        "seq", n_seq, halve_order,
+    )
+    second_normed = finish_norm(hidden_state, second_stats[0], second_stats[1], ln_second_gain)
+    up_part = jnp.dot(second_normed, w_up, preferred_element_type=jnp.float32)
+    (own_up,) = rs_halving((up_part,), "seq", n_seq, halve_order, seq_index, add_parts)
+    own_activated = jax.nn.gelu(own_up, approximate=False).astype(jnp.bfloat16)
+    activated = ag_doubling(own_activated, "seq", n_seq, double_order, seq_index)
     down_part = jnp.dot(activated, w_down, preferred_element_type=jnp.float32)
-    down_sum = lax.psum(down_part.astype(jnp.bfloat16), "tp").astype(jnp.float32)
+    down_sum = ar_doubling(down_part, "tp", n_tp, tp_bits)
     return (hidden_state + down_sum).astype(jnp.bfloat16)
 
 

time: 879 us -> 443 us (0.50)
  blocking collectives: 452 us -> 0 us
  starting transfers between devices: 0.31 us -> 92 us
  waiting for transfers between devices: 359 us -> 279 us
  local copies, waits for them, and re-layouts: 13.4 us -> 29.6 us
  between operations: 13.5 us -> 1.48 us
    psum x4 -> x0, blocking collectives: 379 us -> none  [the longest x1 164 us: body(): full_qkv = lax.psum(partial_qkv, 'seq').astype(jnp.bfloat16)]
    psum x4 -> x0, waiting for transfers between devices: 358 us -> none  [the longest x1 155 us: body(): lax.psum(jnp.dot(second_normed, w_up, preferred_element_type=jnp.float32)...]
    ppermute x0 -> x56, waiting for transfers between devices: none -> 279 us  [the longest x25 138 us: rs_halving(): got = lax.ppermute(send, axis, _pairs(n, bit))]
    ppermute x0 -> x56, starting transfers between devices: none -> 92 us  [the longest x25 46.6 us: rs_halving(): got = lax.ppermute(send, axis, _pairs(n, bit))]
    pmax x1 -> x0, blocking collectives: 72.8 us -> none  [body(): global_top = lax.pmax(local_part[0], 'seq')]
    dynamic_slice x0 -> x20, local copies, waits for them, and re-layouts: none -> 9.16 us  [the longest x9 5.15 us: rs_halving(): lax.dynamic_index_in_dim(p, mine, ax, keepdims=False)]
  transfers between devices with their start and end apart: 4 -> 56, of which waited for: 4 -> 50; matrix products, arithmetic and copies ran while one was open for 0% -> 3% of each run, Pallas kernels for 0% -> 0%
where the time goes in v1:
time: 443 us; the launch traced here: 434 us
  waiting for transfers between devices  279 us (63%)
  starting transfers between devices  92 us (21%)
  local copies, waits for them, and re-layouts  29.6 us (7%)
  other arithmetic  18.5 us (4%)
  matrix products  13 us (3%)
    ppermute x25, waiting for transfers between devices, rs_halving(): got = lax.ppermute(send, axis, _pairs(n, bit))  138 us
    ppermute x15, waiting for transfers between devices, ag_doubling(): got = lax.ppermute(x, axis, _pairs(n, bit))  89.8 us
    ppermute x16, waiting for transfers between devices, ar_doubling(): x = x + lax.ppermute(x, axis, _pairs(n, bit))  51.4 us
    ppermute x25, starting transfers between devices, rs_halving(): got = lax.ppermute(send, axis, _pairs(n, bit))  46.6 us
    ppermute x16, starting transfers between devices, ar_doubling(): x = x + lax.ppermute(x, axis, _pairs(n, bit))  30 us
    ppermute x15, starting transfers between devices, ag_doubling(): got = lax.ppermute(x, axis, _pairs(n, bit))  15.3 us
  transfers between devices with their start and end apart: 56, of which 50 were waited for; matrix products, arithmetic and copies ran while one was open for 3% of the time, Pallas kernels for 0%

profile of v1, /device:TPU:16, one launch (start us, length us, event | category | flops | bytes accessed | tf_op | source)
XLA Modules:
  0.0 433.9 jit_solution(857367880402459027)
XLA Ops:
  13.8 3.3 collective-permute-start.3
  18.6 6.8 %collective-permute-start.4 = (f32[2,384]{1,0:T(2,128)S(1)}, f32[2,384]{1,0:T(2,128)S(1)}, u32[]{:S(2)}, u32[]{:S(2)}) collective-permute-start(f32[2,384]{1,0:T(2,128)S(1)} %add.338), channel_id=1, source_target_pairs={{0,128},{8,136},{16,144},{24,152},{32,160},{40,168},{48,176},{56,1... | collective-permute-start | bytes 9224 | tf_op jit(solution)/shard_map/ppermute | solution.py:44
  34.5 19.1 %collective-permute-done.5 = f32[2,2,2,2,12,1536]{5,3,4,2,1,0:T(2,128)} collective-permute-done((f32[2,2,2,2,12,1536]{5,3,4,2,1,0:T(2,128)}, f32[2,2,2,2,12,1536]{5,3,4,2,1,0:T(2,128)}, u32[]{:S(2)}, u32[]{:S(2)}) %collective-permute-start.5) | collective-permute-done | bytes 1179680 | tf_op jit(solution)/shard_map/ppermute | solution.py:61
  58.6 8.5 %collective-permute-done.6 = f32[2,2,2,12,1536]{4,2,3,1,0:T(2,128)S(1)} collective-permute-done((f32[2,2,2,12,1536]{4,2,3,1,0:T(2,128)S(1)}, f32[2,2,2,12,1536]{4,2,3,1,0:T(2,128)S(1)}, u32[]{:S(2)}, u32[]{:S(2)}) %collective-permute-start.6) | collective-permute-done | bytes 589856 | tf_op jit(solution)/shard_map/ppermute | solution.py:61
  70.7 6.8 %collective-permute-done.7 = f32[2,2,12,1536]{3,1,2,0:T(2,128)S(1)} collective-permute-done((f32[2,2,12,1536]{3,1,2,0:T(2,128)S(1)}, f32[2,2,12,1536]{3,1,2,0:T(2,128)S(1)}, u32[]{:S(2)}, u32[]{:S(2)}) %collective-permute-start.7) | collective-permute-done | bytes 294944 | tf_op jit(solution)/shard_map/ppermute | solution.py:61
  79.6 8.1 %collective-permute-done.8 = f32[2,12,1536]{2,0,1:T(2,128)S(1)} collective-permute-done((f32[2,12,1536]{2,0,1:T(2,128)S(1)}, f32[2,12,1536]{2,0,1:T(2,128)S(1)}, u32[]{:S(2)}, u32[]{:S(2)}) %collective-permute-start.8) | collective-permute-done | bytes 147488 | tf_op jit(solution)/shard_map/ppermute | solution.py:61
  90.9 6.5 %collective-permute-done.9 = f32[12,1536]{1,0:T(8,128)S(1)} collective-permute-done((f32[12,1536]{1,0:T(8,128)S(1)}, f32[12,1536]{1,0:T(8,128)S(1)}, u32[]{:S(2)}, u32[]{:S(2)}) %collective-permute-start.9) | collective-permute-done | bytes 73760 | tf_op jit(solution)/shard_map/ppermute | solution.py:61
  97.4 3.6 collective-permute-start.10
  105.6 4.8 %collective-permute-done.11 = bf16[2,12,512]{2,1,0:T(8,128)(2,1)S(1)} collective-permute-done((bf16[2,12,512]{2,1,0:T(8,128)(2,1)S(1)}, bf16[2,12,512]{2,1,0:T(8,128)(2,1)S(1)}, u32[]{:S(2)}, u32[]{:S(2)}) %collective-permute-start.11) | collective-permute-done | bytes 24608 | tf_op jit(solution)/shard_map/ppermute | solution.py:71
  111.2 5.0 %collective-permute-done.12 = bf16[2,2,12,512]{3,2,1,0:T(8,128)(2,1)S(1)} collective-permute-done((bf16[2,2,12,512]{3,2,1,0:T(8,128)(2,1)S(1)}, bf16[2,2,12,512]{3,2,1,0:T(8,128)(2,1)S(1)}, u32[]{:S(2)}, u32[]{:S(2)}) %collective-permute-start.12) | collective-permute-done | bytes 49184 | tf_op jit(solution)/shard_map/ppermute | solution.py:71
  116.4 4.9 %collective-permute-done.13 = bf16[2,2,2,12,512]{4,3,2,1,0:T(8,128)(2,1)S(1)} collective-permute-done((bf16[2,2,2,12,512]{4,3,2,1,0:T(8,128)(2,1)S(1)}, bf16[2,2,2,12,512]{4,3,2,1,0:T(8,128)(2,1)S(1)}, u32[]{:S(2)}, u32[]{:S(2)}) %collective-permute-start.13) | collective-permute-done | bytes 98336 | tf_op jit(solution)/shard_map/ppermute | solution.py:71
  123.4 4.9 %collective-permute-done.14 = bf16[2,2,2,2,12,512]{5,4,3,2,1,0:T(8,128)(2,1)S(1)} collective-permute-done((bf16[2,2,2,2,12,512]{5,4,3,2,1,0:T(8,128)(2,1)S(1)}, bf16[2,2,2,2,12,512]{5,4,3,2,1,0:T(8,128)(2,1)S(1)}, u32[]{:S(2)}, u32[]{:S(2)}) %collective-permute-start.14) | collective-permute-done | bytes 196640 | tf_op jit(solution)/shard_map/ppermute | solution.py:71
  131.7 4.0 select_reduce_fusion
  152.7 8.9 %collective-permute-start.19 = (f32[2,2,12,4]{2,3,1,0:T(4,128)S(1)}, f32[2,2,12,4]{2,3,1,0:T(4,128)S(1)}, u32[]{:S(2)}, u32[]{:S(2)}) collective-permute-start(f32[2,2,12,4]{2,3,1,0:T(4,128)S(1)} %fusion.79), channel_id=1, source_target_pairs={{0,16},{8,24},{16,0},{24,8},{32,48},{40,56},{48,32},{56,40},{64,80... | collective-permute-start | bytes 2312 | tf_op jit(solution)/shard_map/ppermute | solution.py:61
  161.6 3.5 collective-permute-start.27
  175.6 3.8 collective-permute-done.18
  180.2 5.6 %collective-permute-done.20 = f32[2,2,12,4,128]{4,3,2,1,0:T(4,128)S(1)} collective-permute-done((f32[2,2,12,4,128]{4,3,2,1,0:T(4,128)S(1)}, f32[2,2,12,4,128]{4,3,2,1,0:T(4,128)S(1)}, u32[]{:S(2)}, u32[]{:S(2)}) %collective-permute-start.20) | collective-permute-done | bytes 98336 | tf_op jit(solution)/shard_map/ppermute | solution.py:61
  194.8 3.2 collective-permute-start.24
  202.8 3.2 collective-permute-start.30
  206.0 4.6 %collective-permute-done.30 = bf16[12,512]{1,0:T(8,128)(2,1)S(1)} collective-permute-done((bf16[12,512]{1,0:T(8,128)(2,1)S(1)}, bf16[12,512]{1,0:T(8,128)(2,1)S(1)}, u32[]{:S(2)}, u32[]{:S(2)}) %collective-permute-start.30) | collective-permute-done | bytes 12320 | tf_op jit(solution)/shard_map/ppermute | solution.py:71
  211.2 4.2 collective-permute-done.31
  216.0 5.3 %collective-permute-done.32 = bf16[2,2,12,512]{3,2,1,0:T(8,128)(2,1)S(1)} collective-permute-done((bf16[2,2,12,512]{3,2,1,0:T(8,128)(2,1)S(1)}, bf16[2,2,12,512]{3,2,1,0:T(8,128)(2,1)S(1)}, u32[]{:S(2)}, u32[]{:S(2)}) %collective-permute-start.32) | collective-permute-done | bytes 49184 | tf_op jit(solution)/shard_map/ppermute | solution.py:71
  221.6 4.8 %collective-permute-done.33 = bf16[2,2,2,12,512]{4,3,2,1,0:T(8,128)(2,1)S(1)} collective-permute-done((bf16[2,2,2,12,512]{4,3,2,1,0:T(8,128)(2,1)S(1)}, bf16[2,2,2,12,512]{4,3,2,1,0:T(8,128)(2,1)S(1)}, u32[]{:S(2)}, u32[]{:S(2)}) %collective-permute-start.33) | collective-permute-done | bytes 98336 | tf_op jit(solution)/shard_map/ppermute | solution.py:71
  226.7 6.3 %collective-permute-done.34 = bf16[2,2,2,2,12,512]{5,4,3,2,1,0:T(8,128)(2,1)S(1)} collective-permute-done((bf16[2,2,2,2,12,512]{5,4,3,2,1,0:T(8,128)(2,1)S(1)}, bf16[2,2,2,2,12,512]{5,4,3,2,1,0:T(8,128)(2,1)S(1)}, u32[]{:S(2)}, u32[]{:S(2)}) %collective-permute-start.34) | collective-permute-done | bytes 196640 | tf_op jit(solution)/shard_map/ppermute | solution.py:71
  236.7 5.4 %collective-permute-done.36 = f32[384,128]{0,1:T(8,128)S(1)} collective-permute-done((f32[384,128]{0,1:T(8,128)S(1)}, f32[384,128]{0,1:T(8,128)S(1)}, u32[]{:S(2)}, u32[]{:S(2)}) %collective-permute-start.36) | collective-permute-done | bytes 196640 | tf_op jit(solution)/shard_map/ppermute | solution.py:44
  242.2 3.3 collective-permute-start.37
  245.5 4.6 %collective-permute-done.37 = f32[384,128]{0,1:T(8,128)S(1)} collective-permute-done((f32[384,128]{0,1:T(8,128)S(1)}, f32[384,128]{0,1:T(8,128)S(1)}, u32[]{:S(2)}, u32[]{:S(2)}) %collective-permute-start.37) | collective-permute-done | bytes 196640 | tf_op jit(solution)/shard_map/ppermute | solution.py:44
  250.3 3.5 collective-permute-done.38
  254.1 3.4 collective-permute-done.39
  258.1 4.6 %collective-permute-done.40 = f32[2,384]{1,0:T(2,128)S(1)} collective-permute-done((f32[2,384]{1,0:T(2,128)S(1)}, f32[2,384]{1,0:T(2,128)S(1)}, u32[]{:S(2)}, u32[]{:S(2)}) %collective-permute-start.40) | collective-permute-done | bytes 3104 | tf_op jit(solution)/shard_map/ppermute | solution.py:44
  263.3 3.9 collective-permute-done.41
  270.3 4.4 %collective-permute-done.42 = f32[2,384]{1,0:T(2,128)S(1)} collective-permute-done((f32[2,384]{1,0:T(2,128)S(1)}, f32[2,384]{1,0:T(2,128)S(1)}, u32[]{:S(2)}, u32[]{:S(2)}) %collective-permute-start.42) | collective-permute-done | bytes 3104 | tf_op jit(solution)/shard_map/ppermute | solution.py:44
  277.1 4.6 %reshape.276 = f32[2,2,2,2,2,12,2048]{6,5,4,3,2,1,0:T(8,128)} reshape(f32[384,2048]{1,0:T(8,128)} %fusion.46) | data formatting | bytes 6291456 | tf_op jit(solution)/shard_map/reshape | solution.py:54
  285.6 29.2 %collective-permute-done.43 = f32[2,2,2,2,12,2048]{5,3,4,2,1,0:T(2,128)S(1)} collective-permute-done((f32[2,2,2,2,12,2048]{5,3,4,2,1,0:T(2,128)S(1)}, f32[2,2,2,2,12,2048]{5,3,4,2,1,0:T(2,128)S(1)}, u32[]{:S(2)}, u32[]{:S(2)}) %collective-permute-start.43) | collective-permute-done | bytes 1572896 | tf_op jit(solution)/shard_map/ppermute | solution.py:61
  316.7 11.8 %collective-permute-done.44 = f32[2,2,2,12,2048]{4,2,3,1,0:T(2,128)S(1)} collective-permute-done((f32[2,2,2,12,2048]{4,2,3,1,0:T(2,128)S(1)}, f32[2,2,2,12,2048]{4,2,3,1,0:T(2,128)S(1)}, u32[]{:S(2)}, u32[]{:S(2)}) %collective-permute-start.44) | collective-permute-done | bytes 786464 | tf_op jit(solution)/shard_map/ppermute | solution.py:61
  330.7 8.8 %collective-permute-done.45 = f32[2,2,12,2048]{3,1,2,0:T(2,128)S(1)} collective-permute-done((f32[2,2,12,2048]{3,1,2,0:T(2,128)S(1)}, f32[2,2,12,2048]{3,1,2,0:T(2,128)S(1)}, u32[]{:S(2)}, u32[]{:S(2)}) %collective-permute-start.45) | collective-permute-done | bytes 393248 | tf_op jit(solution)/shard_map/ppermute | solution.py:61
  341.4 9.4 %collective-permute-done.46 = f32[2,12,2048]{2,0,1:T(2,128)S(1)} collective-permute-done((f32[2,12,2048]{2,0,1:T(2,128)S(1)}, f32[2,12,2048]{2,0,1:T(2,128)S(1)}, u32[]{:S(2)}, u32[]{:S(2)}) %collective-permute-start.46) | collective-permute-done | bytes 196640 | tf_op jit(solution)/shard_map/ppermute | solution.py:61
  351.3 3.3 collective-permute-start.47
  354.6 8.3 %collective-permute-done.47 = f32[12,2048]{1,0:T(8,128)S(1)} collective-permute-done((f32[12,2048]{1,0:T(8,128)S(1)}, f32[12,2048]{1,0:T(8,128)S(1)}, u32[]{:S(2)}, u32[]{:S(2)}) %collective-permute-start.47) | collective-permute-done | bytes 98336 | tf_op jit(solution)/shard_map/ppermute | solution.py:61
  363.3 3.3 collective-permute-start.48
  366.6 5.0 %collective-permute-done.48 = bf16[12,2048]{1,0:T(8,128)(2,1)S(1)} collective-permute-done((bf16[12,2048]{1,0:T(8,128)(2,1)S(1)}, bf16[12,2048]{1,0:T(8,128)(2,1)S(1)}, u32[]{:S(2)}, u32[]{:S(2)}) %collective-permute-start.48) | collective-permute-done | bytes 49184 | tf_op jit(solution)/shard_map/ppermute | solution.py:71
  371.7 6.9 %collective-permute-done.49 = bf16[2,12,2048]{2,1,0:T(8,128)(2,1)S(1)} collective-permute-done((bf16[2,12,2048]{2,1,0:T(8,128)(2,1)S(1)}, bf16[2,12,2048]{2,1,0:T(8,128)(2,1)S(1)}, u32[]{:S(2)}, u32[]{:S(2)}) %collective-permute-start.49) | collective-permute-done | bytes 98336 | tf_op jit(solution)/shard_map/ppermute | solution.py:71
  379.2 10.2 %collective-permute-done.50 = bf16[2,2,12,2048]{3,2,0,1:T(8,128)(2,1)S(1)} collective-permute-done((bf16[2,2,12,2048]{3,2,0,1:T(8,128)(2,1)S(1)}, bf16[2,2,12,2048]{3,2,0,1:T(8,128)(2,1)S(1)}, u32[]{:S(2)}, u32[]{:S(2)}) %collective-permute-start.50) | collective-permute-done | bytes 196640 | tf_op jit(solution)/shard_map/ppermute | solution.py:71
  389.7 9.2 %collective-permute-done.51 = bf16[2,2,2,12,2048]{4,3,0,1,2:T(8,128)(2,1)S(1)} collective-permute-done((bf16[2,2,2,12,2048]{4,3,0,1,2:T(8,128)(2,1)S(1)}, bf16[2,2,2,12,2048]{4,3,0,1,2:T(8,128)(2,1)S(1)}, u32[]{:S(2)}, u32[]{:S(2)}) %collective-permute-start.51) | collective-permute-done | bytes 393248 | tf_op jit(solution)/shard_map/ppermute | solution.py:71
  400.0 11.9 %collective-permute-done.52 = bf16[2,2,2,2,12,2048]{5,3,4,2,1,0:T(2,128)(2,1)S(1)} collective-permute-done((bf16[2,2,2,2,12,2048]{5,3,4,2,1,0:T(2,128)(2,1)S(1)}, bf16[2,2,2,2,12,2048]{5,3,4,2,1,0:T(2,128)(2,1)S(1)}, u32[]{:S(2)}, u32[]{:S(2)}) %collective-permute-start.52) | collective-permute-done | bytes 786464 | tf_op jit(solution)/shard_map/ppermute | solution.py:71
  419.5 5.5 %collective-permute-done.54 = f32[384,128]{0,1:T(8,128)S(1)} collective-permute-done((f32[384,128]{0,1:T(8,128)S(1)}, f32[384,128]{0,1:T(8,128)S(1)}, u32[]{:S(2)}, u32[]{:S(2)}) %collective-permute-start.54) | collective-permute-done | bytes 196640 | tf_op jit(solution)/shard_map/ppermute | solution.py:44
  425.0 3.1 collective-permute-start.55
  428.1 4.6 %collective-permute-done.55 = f32[384,128]{0,1:T(8,128)S(1)} collective-permute-done((f32[384,128]{0,1:T(8,128)S(1)}, f32[384,128]{0,1:T(8,128)S(1)}, u32[]{:S(2)}, u32[]{:S(2)}) %collective-permute-start.55) | collective-permute-done | bytes 196640 | tf_op jit(solution)/shard_map/ppermute | solution.py:44
  (291 shorter events, 124.4 us)
Async XLA Ops:
  8.6 5.2 %collective-permute-start.2 = (f32[2,384]{1,0:T(2,128)S(1)}, f32[2,384]{1,0:T(2,128)S(1)}, u32[]{:S(2)}, u32[]{:S(2)}) collective-permute-start(f32[2,384]{1,0:T(2,128)S(1)} %fusion.131), channel_id=1, source_target_pairs={{0,16},{8,24},{16,0},{24,8},{32,48},{40,56},{48,32},{56,40},{64,80... | collective-permute-start | bytes 9224 | tf_op jit(solution)/shard_map/ppermute | solution.py:44
  13.8 4.8 %collective-permute-start.3 = (f32[2,384]{1,0:T(2,128)S(1)}, f32[2,384]{1,0:T(2,128)S(1)}, u32[]{:S(2)}, u32[]{:S(2)}) collective-permute-start(f32[2,384]{1,0:T(2,128)S(1)} %add.337), channel_id=1, source_target_pairs={{0,64},{8,72},{16,80},{24,88},{32,96},{40,104},{48,112},{56,120},{... | collective-permute-start | bytes 9224 | tf_op jit(solution)/shard_map/ppermute | solution.py:44
  18.6 8.7 %collective-permute-start.4 = (f32[2,384]{1,0:T(2,128)S(1)}, f32[2,384]{1,0:T(2,128)S(1)}, u32[]{:S(2)}, u32[]{:S(2)}) collective-permute-start(f32[2,384]{1,0:T(2,128)S(1)} %add.338), channel_id=1, source_target_pairs={{0,128},{8,136},{16,144},{24,152},{32,160},{40,168},{48,176},{56,1... | collective-permute-start | bytes 9224 | tf_op jit(solution)/shard_map/ppermute | solution.py:44
  30.5 23.1 %collective-permute-start.5 = (f32[2,2,2,2,12,1536]{5,3,4,2,1,0:T(2,128)}, f32[2,2,2,2,12,1536]{5,3,4,2,1,0:T(2,128)}, u32[]{:S(2)}, u32[]{:S(2)}) collective-permute-start(f32[2,2,2,2,12,1536]{5,3,4,2,1,0:T(2,128)} %bitcast.335), channel_id=1, source_target_pairs={{0,8},{8,0},{16,24},{24,16},{32,40},{40,32},{48,56},{56,48},{64,72... | collective-permute-start | bytes 3538952 | tf_op jit(solution)/shard_map/ppermute | solution.py:61
  57.1 10.0 %collective-permute-start.6 = (f32[2,2,2,12,1536]{4,2,3,1,0:T(2,128)S(1)}, f32[2,2,2,12,1536]{4,2,3,1,0:T(2,128)S(1)}, u32[]{:S(2)}, u32[]{:S(2)}) collective-permute-start(f32[2,2,2,12,1536]{4,2,3,1,0:T(2,128)S(1)} %dynamic-slice_bitcast_fusion.1), channel_id=1, source_target_pairs={{0,32},{8,40},{16,48},{24,56},{32,0},{40,8},{48,16},{56,24},{64,96... | collective-permute-start | bytes 1769480 | tf_op jit(solution)/shard_map/ppermute | solution.py:61
  69.2 8.3 %collective-permute-start.7 = (f32[2,2,12,1536]{3,1,2,0:T(2,128)S(1)}, f32[2,2,12,1536]{3,1,2,0:T(2,128)S(1)}, u32[]{:S(2)}, u32[]{:S(2)}) collective-permute-start(f32[2,2,12,1536]{3,1,2,0:T(2,128)S(1)} %bitcast.354), channel_id=1, source_target_pairs={{0,16},{8,24},{16,0},{24,8},{32,48},{40,56},{48,32},{56,40},{64,80... | collective-permute-start | bytes 884744 | tf_op jit(solution)/shard_map/ppermute | solution.py:61
  78.1 9.7 %collective-permute-start.8 = (f32[2,12,1536]{2,0,1:T(2,128)S(1)}, f32[2,12,1536]{2,0,1:T(2,128)S(1)}, u32[]{:S(2)}, u32[]{:S(2)}) collective-permute-start(f32[2,12,1536]{2,0,1:T(2,128)S(1)} %bitcast.357), channel_id=1, source_target_pairs={{0,64},{8,72},{16,80},{24,88},{32,96},{40,104},{48,112},{56,120},{... | collective-permute-start | bytes 442376 | tf_op jit(solution)/shard_map/ppermute | solution.py:61
  88.0 9.4 %collective-permute-start.9 = (f32[12,1536]{1,0:T(8,128)S(1)}, f32[12,1536]{1,0:T(8,128)S(1)}, u32[]{:S(2)}, u32[]{:S(2)}) collective-permute-start(f32[12,1536]{1,0:T(8,128)S(1)} %bitcast.359), channel_id=1, source_target_pairs={{0,128},{8,136},{16,144},{24,152},{32,160},{40,168},{48,176},{56,1... | collective-permute-start | bytes 221192 | tf_op jit(solution)/shard_map/ppermute | solution.py:61
  97.4 8.0 %collective-permute-start.10 = (bf16[12,512]{1,0:T(8,128)(2,1)S(1)}, bf16[12,512]{1,0:T(8,128)(2,1)S(1)}, u32[]{:S(2)}, u32[]{:S(2)}) collective-permute-start(bf16[12,512]{1,0:T(8,128)(2,1)S(1)} %slice.40), channel_id=1, source_target_pairs={{0,128},{8,136},{16,144},{24,152},{32,160},{40,168},{48,176},{56,1... | collective-permute-start | bytes 36872 | tf_op jit(solution)/shard_map/ppermute | solution.py:71
  105.5 4.9 %collective-permute-start.11 = (bf16[2,12,512]{2,1,0:T(8,128)(2,1)S(1)}, bf16[2,12,512]{2,1,0:T(8,128)(2,1)S(1)}, u32[]{:S(2)}, u32[]{:S(2)}) collective-permute-start(bf16[2,12,512]{2,1,0:T(8,128)(2,1)S(1)} %pad_maximum_fusion.13), channel_id=1, source_target_pairs={{0,64},{8,72},{16,80},{24,88},{32,96},{40,104},{48,112},{56,120},{... | collective-permute-start | bytes 73736 | tf_op jit(solution)/shard_map/ppermute | solution.py:71
  110.4 5.9 %collective-permute-start.12 = (bf16[2,2,12,512]{3,2,1,0:T(8,128)(2,1)S(1)}, bf16[2,2,12,512]{3,2,1,0:T(8,128)(2,1)S(1)}, u32[]{:S(2)}, u32[]{:S(2)}) collective-permute-start(bf16[2,2,12,512]{3,2,1,0:T(8,128)(2,1)S(1)} %pad_maximum_fusion.11), channel_id=1, source_target_pairs={{0,16},{8,24},{16,0},{24,8},{32,48},{40,56},{48,32},{56,40},{64,80... | collective-permute-start | bytes 147464 | tf_op jit(solution)/shard_map/ppermute | solution.py:71
  116.3 5.1 %collective-permute-start.13 = (bf16[2,2,2,12,512]{4,3,2,1,0:T(8,128)(2,1)S(1)}, bf16[2,2,2,12,512]{4,3,2,1,0:T(8,128)(2,1)S(1)}, u32[]{:S(2)}, u32[]{:S(2)}) collective-permute-start(bf16[2,2,2,12,512]{4,3,2,1,0:T(8,128)(2,1)S(1)} %pad_maximum_fusion.8), channel_id=1, source_target_pairs={{0,32},{8,40},{16,48},{24,56},{32,0},{40,8},{48,16},{56,24},{64,96... | collective-permute-start | bytes 294920 | tf_op jit(solution)/shard_map/ppermute | solution.py:71
  121.4 6.8 %collective-permute-start.14 = (bf16[2,2,2,2,12,512]{5,4,3,2,1,0:T(8,128)(2,1)S(1)}, bf16[2,2,2,2,12,512]{5,4,3,2,1,0:T(8,128)(2,1)S(1)}, u32[]{:S(2)}, u32[]{:S(2)}) collective-permute-start(bf16[2,2,2,2,12,512]{5,4,3,2,1,0:T(8,128)(2,1)S(1)} %pad_maximum_fusion.5), channel_id=1, source_target_pairs={{0,8},{8,0},{16,24},{24,16},{32,40},{40,32},{48,56},{56,48},{64,72... | collective-permute-start | bytes 589832 | tf_op jit(solution)/shard_map/ppermute | solution.py:71
  140.3 5.7 %collective-permute-start.25 = (f32[2,2,2,2,12,4]{4,5,3,2,1,0:T(4,128)S(1)}, f32[2,2,2,2,12,4]{4,5,3,2,1,0:T(4,128)S(1)}, u32[]{:S(2)}, u32[]{:S(2)}) collective-permute-start(f32[2,2,2,2,12,4]{4,5,3,2,1,0:T(4,128)S(1)} %bitcast.366), channel_id=1, source_target_pairs={{0,8},{8,0},{16,24},{24,16},{32,40},{40,32},{48,56},{56,48},{64,72... | collective-permute-start | bytes 9224 | tf_op jit(solution)/shard_map/ppermute | solution.py:61
  144.2 4.3 %collective-permute-start.15 = (f32[2,2,2,2,12,4]{4,5,3,2,1,0:T(4,128)S(1)}, f32[2,2,2,2,12,4]{4,5,3,2,1,0:T(4,128)S(1)}, u32[]{:S(2)}, u32[]{:S(2)}) collective-permute-start(f32[2,2,2,2,12,4]{4,5,3,2,1,0:T(4,128)S(1)} %bitcast.367), channel_id=1, source_target_pairs={{0,8},{8,0},{16,24},{24,16},{32,40},{40,32},{48,56},{56,48},{64,72... | collective-permute-start | bytes 9224 | tf_op jit(solution)/shard_map/ppermute | solution.py:61
  152.7 14.1 %collective-permute-start.19 = (f32[2,2,12,4]{2,3,1,0:T(4,128)S(1)}, f32[2,2,12,4]{2,3,1,0:T(4,128)S(1)}, u32[]{:S(2)}, u32[]{:S(2)}) collective-permute-start(f32[2,2,12,4]{2,3,1,0:T(4,128)S(1)} %fusion.79), channel_id=1, source_target_pairs={{0,16},{8,24},{16,0},{24,8},{32,48},{40,56},{48,32},{56,40},{64,80... | collective-permute-start | bytes 2312 | tf_op jit(solution)/shard_map/ppermute | solution.py:61
  161.6 5.2 %collective-permute-start.27 = (f32[2,2,12,4]{2,3,1,0:T(4,128)S(1)}, f32[2,2,12,4]{2,3,1,0:T(4,128)S(1)}, u32[]{:S(2)}, u32[]{:S(2)}) collective-permute-start(f32[2,2,12,4]{2,3,1,0:T(4,128)S(1)} %fusion.83), channel_id=1, source_target_pairs={{0,16},{8,24},{16,0},{24,8},{32,48},{40,56},{48,32},{56,40},{64,80... | collective-permute-start | bytes 2312 | tf_op jit(solution)/shard_map/ppermute | solution.py:61
  165.3 7.8 %collective-permute-start.16 = (f32[2,2,2,2,12,4,128]{6,5,4,3,2,1,0:T(4,128)S(1)}, f32[2,2,2,2,12,4,128]{6,5,4,3,2,1,0:T(4,128)S(1)}, u32[]{:S(2)}, u32[]{:S(2)}) collective-permute-start(f32[2,2,2,2,12,4,128]{6,5,4,3,2,1,0:T(4,128)S(1)} %dynamic-slice_bitcast_fusion.2), channel_id=1, source_target_pairs={{0,8},{8,0},{16,24},{24,16},{32,40},{40,32},{48,56},{56,48},{64,72... | collective-permute-start | bytes 1179656 | tf_op jit(solution)/shard_map/ppermute | solution.py:61
  166.9 8.7 %collective-permute-start.21 = (f32[2,12,4]{1,2,0:T(4,128)S(1)}, f32[2,12,4]{1,2,0:T(4,128)S(1)}, u32[]{:S(2)}, u32[]{:S(2)}) collective-permute-start(f32[2,12,4]{1,2,0:T(4,128)S(1)} %fusion.86), channel_id=1, source_target_pairs={{0,64},{8,72},{16,80},{24,88},{32,96},{40,104},{48,112},{56,120},{... | collective-permute-start | bytes 1160 | tf_op jit(solution)/shard_map/ppermute | solution.py:61
  169.3 6.2 %collective-permute-start.28 = (f32[2,12,4]{1,2,0:T(4,128)S(1)}, f32[2,12,4]{1,2,0:T(4,128)S(1)}, u32[]{:S(2)}, u32[]{:S(2)}) collective-permute-start(f32[2,12,4]{1,2,0:T(4,128)S(1)} %fusion.90), channel_id=1, source_target_pairs={{0,64},{8,72},{16,80},{24,88},{32,96},{40,104},{48,112},{56,120},{... | collective-permute-start | bytes 1160 | tf_op jit(solution)/shard_map/ppermute | solution.py:61
  173.6 5.8 %collective-permute-start.18 = (f32[2,2,2,12,4,128]{5,4,3,1,0,2:T(4,128)S(1)}, f32[2,2,2,12,4,128]{5,4,3,1,0,2:T(4,128)S(1)}, u32[]{:S(2)}, u32[]{:S(2)}) collective-permute-start(f32[2,2,2,12,4,128]{5,4,3,1,0,2:T(4,128)S(1)} %bitcast.355), channel_id=1, source_target_pairs={{0,32},{8,40},{16,48},{24,56},{32,0},{40,8},{48,16},{56,24},{64,96... | collective-permute-start | bytes 589832 | tf_op jit(solution)/shard_map/ppermute | solution.py:61
  179.7 6.2 %collective-permute-start.20 = (f32[2,2,12,4,128]{4,3,2,1,0:T(4,128)S(1)}, f32[2,2,12,4,128]{4,3,2,1,0:T(4,128)S(1)}, u32[]{:S(2)}, u32[]{:S(2)}) collective-permute-start(f32[2,2,12,4,128]{4,3,2,1,0:T(4,128)S(1)} %dynamic-slice_bitcast_fusion.3), channel_id=1, source_target_pairs={{0,16},{8,24},{16,0},{24,8},{32,48},{40,56},{48,32},{56,40},{64,80... | collective-permute-start | bytes 294920 | tf_op jit(solution)/shard_map/ppermute | solution.py:61
  186.1 8.6 %collective-permute-start.22 = (f32[2,12,4,128]{3,2,1,0:T(4,128)S(1)}, f32[2,12,4,128]{3,2,1,0:T(4,128)S(1)}, u32[]{:S(2)}, u32[]{:S(2)}) collective-permute-start(f32[2,12,4,128]{3,2,1,0:T(4,128)S(1)} %dynamic-slice_bitcast_fusion.4), channel_id=1, source_target_pairs={{0,64},{8,72},{16,80},{24,88},{32,96},{40,104},{48,112},{56,120},{... | collective-permute-start | bytes 147464 | tf_op jit(solution)/shard_map/ppermute | solution.py:61
  188.5 9.5 %collective-permute-start.23 = (f32[12,4]{0,1:T(4,128)S(1)}, f32[12,4]{0,1:T(4,128)S(1)}, u32[]{:S(2)}, u32[]{:S(2)}) collective-permute-start(f32[12,4]{0,1:T(4,128)S(1)} %fusion.95), channel_id=1, source_target_pairs={{0,128},{8,136},{16,144},{24,152},{32,160},{40,168},{48,176},{56,1... | collective-permute-start | bytes 584 | tf_op jit(solution)/shard_map/ppermute | solution.py:61
  191.6 7.5 %collective-permute-start.29 = (f32[12,4]{0,1:T(4,128)S(1)}, f32[12,4]{0,1:T(4,128)S(1)}, u32[]{:S(2)}, u32[]{:S(2)}) collective-permute-start(f32[12,4]{0,1:T(4,128)S(1)} %fusion.101), channel_id=1, source_target_pairs={{0,128},{8,136},{16,144},{24,152},{32,160},{40,168},{48,176},{56,1... | collective-permute-start | bytes 584 | tf_op jit(solution)/shard_map/ppermute | solution.py:61
  194.8 7.8 %collective-permute-start.24 = (f32[12,4,128]{2,1,0:T(4,128)S(1)}, f32[12,4,128]{2,1,0:T(4,128)S(1)}, u32[]{:S(2)}, u32[]{:S(2)}) collective-permute-start(f32[12,4,128]{2,1,0:T(4,128)S(1)} %dynamic-slice_bitcast_fusion.5), channel_id=1, source_target_pairs={{0,128},{8,136},{16,144},{24,152},{32,160},{40,168},{48,176},{56,1... | collective-permute-start | bytes 73736 | tf_op jit(solution)/shard_map/ppermute | solution.py:61
  202.8 7.7 %collective-permute-start.30 = (bf16[12,512]{1,0:T(8,128)(2,1)S(1)}, bf16[12,512]{1,0:T(8,128)(2,1)S(1)}, u32[]{:S(2)}, u32[]{:S(2)}) collective-permute-start(bf16[12,512]{1,0:T(8,128)(2,1)S(1)} %bitcast.364), channel_id=1, source_target_pairs={{0,128},{8,136},{16,144},{24,152},{32,160},{40,168},{48,176},{56,1... | collective-permute-start | bytes 36872 | tf_op jit(solution)/shard_map/ppermute | solution.py:71
  210.5 4.9 %collective-permute-start.31 = (bf16[2,12,512]{2,1,0:T(8,128)(2,1)S(1)}, bf16[2,12,512]{2,1,0:T(8,128)(2,1)S(1)}, u32[]{:S(2)}, u32[]{:S(2)}) collective-permute-start(bf16[2,12,512]{2,1,0:T(8,128)(2,1)S(1)} %pad_maximum_fusion.14), channel_id=1, source_target_pairs={{0,64},{8,72},{16,80},{24,88},{32,96},{40,104},{48,112},{56,120},{... | collective-permute-start | bytes 73736 | tf_op jit(solution)/shard_map/ppermute | solution.py:71
  215.5 5.9 %collective-permute-start.32 = (bf16[2,2,12,512]{3,2,1,0:T(8,128)(2,1)S(1)}, bf16[2,2,12,512]{3,2,1,0:T(8,128)(2,1)S(1)}, u32[]{:S(2)}, u32[]{:S(2)}) collective-permute-start(bf16[2,2,12,512]{3,2,1,0:T(8,128)(2,1)S(1)} %pad_maximum_fusion.12), channel_id=1, source_target_pairs={{0,16},{8,24},{16,0},{24,8},{32,48},{40,56},{48,32},{56,40},{64,80... | collective-permute-start | bytes 147464 | tf_op jit(solution)/shard_map/ppermute | solution.py:71
  221.4 5.1 %collective-permute-start.33 = (bf16[2,2,2,12,512]{4,3,2,1,0:T(8,128)(2,1)S(1)}, bf16[2,2,2,12,512]{4,3,2,1,0:T(8,128)(2,1)S(1)}, u32[]{:S(2)}, u32[]{:S(2)}) collective-permute-start(bf16[2,2,2,12,512]{4,3,2,1,0:T(8,128)(2,1)S(1)} %pad_maximum_fusion.9), channel_id=1, source_target_pairs={{0,32},{8,40},{16,48},{24,56},{32,0},{40,8},{48,16},{56,24},{64,96... | collective-permute-start | bytes 294920 | tf_op jit(solution)/shard_map/ppermute | solution.py:71
  226.5 6.5 %collective-permute-start.34 = (bf16[2,2,2,2,12,512]{5,4,3,2,1,0:T(8,128)(2,1)S(1)}, bf16[2,2,2,2,12,512]{5,4,3,2,1,0:T(8,128)(2,1)S(1)}, u32[]{:S(2)}, u32[]{:S(2)}) collective-permute-start(bf16[2,2,2,2,12,512]{5,4,3,2,1,0:T(8,128)(2,1)S(1)} %pad_maximum_fusion.6), channel_id=1, source_target_pairs={{0,8},{8,0},{16,24},{24,16},{32,40},{40,32},{48,56},{56,48},{64,72... | collective-permute-start | bytes 589832 | tf_op jit(solution)/shard_map/ppermute | solution.py:71
  235.1 7.0 %collective-permute-start.36 = (f32[384,128]{0,1:T(8,128)S(1)}, f32[384,128]{0,1:T(8,128)S(1)}, u32[]{:S(2)}, u32[]{:S(2)}) collective-permute-start(f32[384,128]{0,1:T(8,128)S(1)} %add.387), channel_id=1, source_target_pairs={{0,2},{1,3},{2,0},{3,1},{4,6},{5,7},{6,4},{7,5},{8,10},{9,11},{10,... | collective-permute-start | bytes 589832 | tf_op jit(solution)/shard_map/ppermute | solution.py:44
  242.2 7.9 %collective-permute-start.37 = (f32[384,128]{0,1:T(8,128)S(1)}, f32[384,128]{0,1:T(8,128)S(1)}, u32[]{:S(2)}, u32[]{:S(2)}) collective-permute-start(f32[384,128]{0,1:T(8,128)S(1)} %add.388), channel_id=1, source_target_pairs={{0,4},{1,5},{2,6},{3,7},{4,0},{5,1},{6,2},{7,3},{8,12},{9,13},{10,... | collective-permute-start | bytes 589832 | tf_op jit(solution)/shard_map/ppermute | solution.py:44
  257.5 5.2 %collective-permute-start.40 = (f32[2,384]{1,0:T(2,128)S(1)}, f32[2,384]{1,0:T(2,128)S(1)}, u32[]{:S(2)}, u32[]{:S(2)}) collective-permute-start(f32[2,384]{1,0:T(2,128)S(1)} %fusion.130), channel_id=1, source_target_pairs={{0,16},{8,24},{16,0},{24,8},{32,48},{40,56},{48,32},{56,40},{64,80... | collective-permute-start | bytes 9224 | tf_op jit(solution)/shard_map/ppermute | solution.py:44
  262.7 4.5 %collective-permute-start.41 = (f32[2,384]{1,0:T(2,128)S(1)}, f32[2,384]{1,0:T(2,128)S(1)}, u32[]{:S(2)}, u32[]{:S(2)}) collective-permute-start(f32[2,384]{1,0:T(2,128)S(1)} %add.393), channel_id=1, source_target_pairs={{0,64},{8,72},{16,80},{24,88},{32,96},{40,104},{48,112},{56,120},{... | collective-permute-start | bytes 9224 | tf_op jit(solution)/shard_map/ppermute | solution.py:44
  267.2 7.5 %collective-permute-start.42 = (f32[2,384]{1,0:T(2,128)S(1)}, f32[2,384]{1,0:T(2,128)S(1)}, u32[]{:S(2)}, u32[]{:S(2)}) collective-permute-start(f32[2,384]{1,0:T(2,128)S(1)} %add.394), channel_id=1, source_target_pairs={{0,128},{8,136},{16,144},{24,152},{32,160},{40,168},{48,176},{56,1... | collective-permute-start | bytes 9224 | tf_op jit(solution)/shard_map/ppermute | solution.py:44
  285.4 29.4 %collective-permute-start.43 = (f32[2,2,2,2,12,2048]{5,3,4,2,1,0:T(2,128)S(1)}, f32[2,2,2,2,12,2048]{5,3,4,2,1,0:T(2,128)S(1)}, u32[]{:S(2)}, u32[]{:S(2)}) collective-permute-start(f32[2,2,2,2,12,2048]{5,3,4,2,1,0:T(2,128)S(1)} %bitcast.348), channel_id=1, source_target_pairs={{0,8},{8,0},{16,24},{24,16},{32,40},{40,32},{48,56},{56,48},{64,72... | collective-permute-start | bytes 4718600 | tf_op jit(solution)/shard_map/ppermute | solution.py:61
  316.4 12.1 %collective-permute-start.44 = (f32[2,2,2,12,2048]{4,2,3,1,0:T(2,128)S(1)}, f32[2,2,2,12,2048]{4,2,3,1,0:T(2,128)S(1)}, u32[]{:S(2)}, u32[]{:S(2)}) collective-permute-start(f32[2,2,2,12,2048]{4,2,3,1,0:T(2,128)S(1)} %dynamic-slice_bitcast_fusion), channel_id=1, source_target_pairs={{0,32},{8,40},{16,48},{24,56},{32,0},{40,8},{48,16},{56,24},{64,96... | collective-permute-start | bytes 2359304 | tf_op jit(solution)/shard_map/ppermute | solution.py:61
  330.1 9.4 %collective-permute-start.45 = (f32[2,2,12,2048]{3,1,2,0:T(2,128)S(1)}, f32[2,2,12,2048]{3,1,2,0:T(2,128)S(1)}, u32[]{:S(2)}, u32[]{:S(2)}) collective-permute-start(f32[2,2,12,2048]{3,1,2,0:T(2,128)S(1)} %bitcast.353), channel_id=1, source_target_pairs={{0,16},{8,24},{16,0},{24,8},{32,48},{40,56},{48,32},{56,40},{64,80... | collective-permute-start | bytes 1179656 | tf_op jit(solution)/shard_map/ppermute | solution.py:61
  340.5 10.3 %collective-permute-start.46 = (f32[2,12,2048]{2,0,1:T(2,128)S(1)}, f32[2,12,2048]{2,0,1:T(2,128)S(1)}, u32[]{:S(2)}, u32[]{:S(2)}) collective-permute-start(f32[2,12,2048]{2,0,1:T(2,128)S(1)} %bitcast.356), channel_id=1, source_target_pairs={{0,64},{8,72},{16,80},{24,88},{32,96},{40,104},{48,112},{56,120},{... | collective-permute-start | bytes 589832 | tf_op jit(solution)/shard_map/ppermute | solution.py:61
  351.3 11.7 %collective-permute-start.47 = (f32[12,2048]{1,0:T(8,128)S(1)}, f32[12,2048]{1,0:T(8,128)S(1)}, u32[]{:S(2)}, u32[]{:S(2)}) collective-permute-start(f32[12,2048]{1,0:T(8,128)S(1)} %bitcast.358), channel_id=1, source_target_pairs={{0,128},{8,136},{16,144},{24,152},{32,160},{40,168},{48,176},{56,1... | collective-permute-start | bytes 294920 | tf_op jit(solution)/shard_map/ppermute | solution.py:61
  363.3 8.3 %collective-permute-start.48 = (bf16[12,2048]{1,0:T(8,128)(2,1)S(1)}, bf16[12,2048]{1,0:T(8,128)(2,1)S(1)}, u32[]{:S(2)}, u32[]{:S(2)}) collective-permute-start(bf16[12,2048]{1,0:T(8,128)(2,1)S(1)} %fusion.38), channel_id=1, source_target_pairs={{0,128},{8,136},{16,144},{24,152},{32,160},{40,168},{48,176},{56,1... | collective-permute-start | bytes 147464 | tf_op jit(solution)/shard_map/ppermute | solution.py:71
  371.6 7.0 %collective-permute-start.49 = (bf16[2,12,2048]{2,1,0:T(8,128)(2,1)S(1)}, bf16[2,12,2048]{2,1,0:T(8,128)(2,1)S(1)}, u32[]{:S(2)}, u32[]{:S(2)}) collective-permute-start(bf16[2,12,2048]{2,1,0:T(8,128)(2,1)S(1)} %pad_maximum_fusion.10), channel_id=1, source_target_pairs={{0,64},{8,72},{16,80},{24,88},{32,96},{40,104},{48,112},{56,120},{... | collective-permute-start | bytes 294920 | tf_op jit(solution)/shard_map/ppermute | solution.py:71
  378.6 10.8 %collective-permute-start.50 = (bf16[2,2,12,2048]{3,2,0,1:T(8,128)(2,1)S(1)}, bf16[2,2,12,2048]{3,2,0,1:T(8,128)(2,1)S(1)}, u32[]{:S(2)}, u32[]{:S(2)}) collective-permute-start(bf16[2,2,12,2048]{3,2,0,1:T(8,128)(2,1)S(1)} %pad_maximum_fusion.7), channel_id=1, source_target_pairs={{0,16},{8,24},{16,0},{24,8},{32,48},{40,56},{48,32},{56,40},{64,80... | collective-permute-start | bytes 589832 | tf_op jit(solution)/shard_map/ppermute | solution.py:71
  389.6 9.3 %collective-permute-start.51 = (bf16[2,2,2,12,2048]{4,3,0,1,2:T(8,128)(2,1)S(1)}, bf16[2,2,2,12,2048]{4,3,0,1,2:T(8,128)(2,1)S(1)}, u32[]{:S(2)}, u32[]{:S(2)}) collective-permute-start(bf16[2,2,2,12,2048]{4,3,0,1,2:T(8,128)(2,1)S(1)} %pad_maximum_fusion.4), channel_id=1, source_target_pairs={{0,32},{8,40},{16,48},{24,56},{32,0},{40,8},{48,16},{56,24},{64,96... | collective-permute-start | bytes 1179656 | tf_op jit(solution)/shard_map/ppermute | solution.py:71
  399.9 12.1 %collective-permute-start.52 = (bf16[2,2,2,2,12,2048]{5,3,4,2,1,0:T(2,128)(2,1)S(1)}, bf16[2,2,2,2,12,2048]{5,3,4,2,1,0:T(2,128)(2,1)S(1)}, u32[]{:S(2)}, u32[]{:S(2)}) collective-permute-start(bf16[2,2,2,2,12,2048]{5,3,4,2,1,0:T(2,128)(2,1)S(1)} %copy.593), channel_id=1, source_target_pairs={{0,8},{8,0},{16,24},{24,16},{32,40},{40,32},{48,56},{56,48},{64,72... | collective-permute-start | bytes 2359304 | tf_op jit(solution)/shard_map/ppermute | solution.py:71
  418.0 7.0 %collective-permute-start.54 = (f32[384,128]{0,1:T(8,128)S(1)}, f32[384,128]{0,1:T(8,128)S(1)}, u32[]{:S(2)}, u32[]{:S(2)}) collective-permute-start(f32[384,128]{0,1:T(8,128)S(1)} %add.402), channel_id=1, source_target_pairs={{0,2},{1,3},{2,0},{3,1},{4,6},{5,7},{6,4},{7,5},{8,10},{9,11},{10,... | collective-permute-start | bytes 589832 | tf_op jit(solution)/shard_map/ppermute | solution.py:44
  425.0 7.7 %collective-permute-start.55 = (f32[384,128]{0,1:T(8,128)S(1)}, f32[384,128]{0,1:T(8,128)S(1)}, u32[]{:S(2)}, u32[]{:S(2)}) collective-permute-start(f32[384,128]{0,1:T(8,128)S(1)} %add.403), channel_id=1, source_target_pairs={{0,4},{1,5},{2,6},{3,7},{4,0},{5,1},{6,2},{7,3},{8,12},{9,13},{10,... | collective-permute-start | bytes 589832 | tf_op jit(solution)/shard_map/ppermute | solution.py:44
  (18 other events, 343.7 us)
